TPU v7x, 256 devices: a whole 4x4x8 slice. The times are simulated.
256 devices in a mesh: ta: 4 (over y), gz: 8 (over x, core), xy: 8 (over z).
Axes of the slice: x: 4, y: 4, z: 8, core: 2. Of those that a mesh axis runs over, the one named last changes fastest.
Arguments:
- right_side: bfloat16 [8, 16, 16, 2, 16, 128], P('ta', 'gz', 'xy'), may hold values from -40 to 40
- links: bfloat16 [8, 16, 16, 2, 9, 64, 128], P('ta', 'gz', 'xy'), may hold values from -4 to 8, as said below
Outputs:
- solution: float32 [8, 16, 16, 2, 16, 128], P('ta', 'gz', 'xy')
Inputs may be any that keep to these rules, and one draw needn't show every extreme that they name: `links`: block entries; block 0 acts on the site itself.
All inputs are finite; a program needn't handle non-finite values.
Results may differ from a plain program's by a relative error of at most 0.008.
Values may be sent and summed in bfloat16 or wider, within the bound.
No kernel may reach another device: no remote copies, remote signals or barrier semaphores. Data moves between devices by JAX's collectives and lax.ppermute only.
A program may use at most 64 MiB of HBM per device.

v0:
```python
import jax
import jax.numpy as jnp
from jax import lax
from jax.sharding import PartitionSpec as P

ITERS = 3
EPSILON = 1e-06


def extended(value, sides, width):
    for axis, dim in sides:
        size, length = (lax.axis_size(axis), value.shape[dim])
        up = [(i, (i + 1) % size) for i in range(size)]
        down = [(j, i) for i, j in up]
        last = lax.slice_in_dim(value, length - width, length, axis=dim)
        first = lax.slice_in_dim(value, 0, width, axis=dim)
        before = lax.ppermute(last, axis, up)
        after = lax.ppermute(first, axis, down)
        value = jnp.concatenate([before, value, after], axis=dim)
    return value


def turned(field):
    half = field.shape[-1] // 2
    return jnp.concatenate([-field[..., half:], field[..., :half]], axis=-1)


def inner_pair(left, right):
    return (
        jnp.sum(left * right, axis=(0, 1, 2, 3, 5)),
        jnp.sum(turned(left) * right, axis=(0, 1, 2, 3, 5)),
    )


def combined(coef_re, coef_im, field):
    return coef_re[:, None] * field + coef_im[:, None] * turned(field)


def global_squares(field):
    return lax.psum(jnp.sum(field * field, axis=(0, 1, 2, 3, 5)), ("ta", "gz", "xy"))


def hop_products(padded, blocks, half):
    here = padded[1:-1, 1:-1, 1:-1]
    near = jnp.stack(
        [
            here,
            padded[2:, 1:-1, 1:-1],
            padded[:-2, 1:-1, 1:-1],
            padded[1:-1, 2:, 1:-1],
            padded[1:-1, :-2, 1:-1],
            padded[1:-1, 1:-1, 2:],
            padded[1:-1, 1:-1, :-2],
            jnp.roll(here, -1, 3),
            jnp.roll(here, 1, 3),
        ],
        axis=0,
    )
    real_half = near[..., :half]
    imag_half = near[..., half:]
    paired = jnp.stack(
        [
            jnp.concatenate([real_half, -imag_half], axis=-1),
            jnp.concatenate([imag_half, real_half], axis=-1),
        ],
        axis=-3,
    )
    paired = paired.reshape(9, blocks.shape[0], 2, here.shape[4], here.shape[5])
    output = jnp.einsum("sbkj,bscrj->srck", blocks, paired, preferred_element_type=jnp.float32)
    return output.reshape(here.shape).astype(jnp.bfloat16)


def least_squares(rows_re, rows_im, start_norm):
    count = len(rows_re[0])
    height_re = jnp.transpose(jnp.stack([jnp.stack(row) for row in rows_re]), (2, 0, 1))
    height_im = jnp.transpose(jnp.stack([jnp.stack(row) for row in rows_im]), (2, 0, 1))
    upper = jnp.concatenate([height_re, -height_im], axis=2)
    lower = jnp.concatenate([height_im, height_re], axis=2)
    stacked = jnp.concatenate([upper, lower], axis=1)
    normal = jnp.einsum("rik,rij->rkj", stacked, stacked, precision=lax.Precision.HIGHEST)
    target = start_norm[:, None] * stacked[:, 0, :]
    factor = jnp.linalg.cholesky(normal)
    middle = lax.linalg.triangular_solve(factor, target[:, :, None], left_side=True, lower=True)
    coefs = lax.linalg.triangular_solve(
        factor, middle, left_side=True, lower=True, transpose_a=True
    )[:, :, 0]
    return (coefs[:, :count], coefs[:, count:])


def on_device(right_side, links):
    dims = right_side.shape
    half = dims[5] // 2
    sites = dims[0] * dims[1] * dims[2] * dims[3]
    blocks = links.reshape(sites, 9, half, dims[5])
    source = right_side.astype(jnp.float32)
    start_norm = jnp.sqrt(global_squares(source) + EPSILON)
    basis = [source / start_norm[:, None]]
    zero_row = jnp.zeros_like(start_norm)
    rows_re = [[zero_row for column in range(ITERS)] for height in range(ITERS + 1)]
    rows_im = [[zero_row for column in range(ITERS)] for height in range(ITERS + 1)]
    for column in range(ITERS):
        padded = extended(basis[column].astype(jnp.bfloat16), (("ta", 0), ("gz", 1), ("xy", 2)), 1)
        residue = hop_products(padded, blocks, half).astype(jnp.float32)
        for earlier in range(column + 1):
            proj_re, proj_im = lax.psum(inner_pair(basis[earlier], residue), ("ta", "gz", "xy"))
            rows_re[earlier][column] = proj_re
            rows_im[earlier][column] = proj_im
            residue = residue - combined(proj_re, proj_im, basis[earlier])
        length = jnp.sqrt(global_squares(residue) + EPSILON)
        rows_re[column + 1][column] = length
        if column + 1 < ITERS:
            basis.append(residue / length[:, None])
    coef_re, coef_im = least_squares(rows_re, rows_im, start_norm)
    solution = jnp.zeros(dims, jnp.float32)
    for column in range(ITERS):
        solution = solution + combined(coef_re[:, column], coef_im[:, column], basis[column])
    return solution


def solution(mesh):
    in_specs = (P("ta", "gz", "xy", None, None, None), P("ta", "gz", "xy", None, None, None, None))
    out_specs = P("ta", "gz", "xy", None, None, None)
    return jax.shard_map(
        on_device, mesh=mesh, in_specs=in_specs, out_specs=out_specs, check_vma=False
    )
```

profile of v0, /device:TPU:1, one launch (start us, length us, event | category | flops | bytes accessed | tf_op | source)
XLA Modules:
  0.0 832.7 jit_solution(8448418020664260992)
XLA Ops:
  1.1 81.4 %psum.112 = f32[16]{0:T(128)S(1)} all-reduce(f32[16]{0:T(128)S(1)} %fusion.48), channel_id=1, replica_groups=mesh['ta'=4,'gz'=8,'xy'=8] {'ta','gz','xy'}, use_global_device_ids=true, to_apply=%region_1.0 | all-reduce | flops 16 | bytes 128 | tf_op jit(solution)/shard_map/psum | solution.py:40
  88.1 2.1 collective-permute-start.2
  94.9 2.3 collective-permute-done.4
  102.2 74.0 %all-reduce.7 = (f32[16]{0:T(128)S(1)}, f32[16]{0:T(128)S(1)}) all-reduce(f32[16]{0:T(128)S(1)} %multiply_reduce_fusion.2, f32[16]{0:T(128)S(1)} %get-tuple-element.74), channel_id=1, replica_groups=mesh['ta'=4,'gz'=8,'xy'=8] {'ta','gz','xy'}, use_global_device_ids=true, to_apply=%region_5.6 | all-reduce | flops 32 | bytes 256 | tf_op jit(solution)/shard_map/psum | solution.py:105
  176.4 74.4 %psum.115 = f32[16]{0:T(128)S(1)} all-reduce(f32[16]{0:T(128)S(1)} %get-tuple-element.37), channel_id=1, replica_groups=mesh['ta'=4,'gz'=8,'xy'=8] {'ta','gz','xy'}, use_global_device_ids=true, to_apply=%region_7.8 | all-reduce | flops 16 | bytes 128 | tf_op jit(solution)/shard_map/psum | solution.py:40
  250.9 2.3 collective-permute-start.6
  254.2 3.0 collective-permute-done.7
  257.2 2.1 collective-permute-start.8
  262.6 2.3 collective-permute-done.10
  264.9 2.1 collective-permute-done.11
  269.7 75.2 %all-reduce.6 = (f32[16]{0:T(128)S(1)}, f32[16]{0:T(128)S(1)}) all-reduce(f32[16]{0:T(128)S(1)} %get-tuple-element.100, f32[16]{0:T(128)S(1)} %multiply_reduce_fusion.12), channel_id=1, replica_groups=mesh['ta'=4,'gz'=8,'xy'=8] {'ta','gz','xy'}, use_global_device_ids=true, to_apply=%region_11.12 | all-reduce | flops 32 | bytes 256 | tf_op jit(solution)/shard_map/psum | solution.py:105
  346.0 74.4 %all-reduce.5 = (f32[16]{0:T(128)S(1)}, f32[16]{0:T(128)S(1)}) all-reduce(f32[16]{0:T(128)S(1)} %get-tuple-element.10, f32[16]{0:T(128)S(1)} %get-tuple-element.9), channel_id=1, replica_groups=mesh['ta'=4,'gz'=8,'xy'=8] {'ta','gz','xy'}, use_global_device_ids=true, to_apply=%region_15.16 | all-reduce | flops 32 | bytes 256 | tf_op jit(solution)/shard_map/psum | solution.py:105
  420.6 73.4 %psum.120 = f32[16]{0:T(128)S(1)} all-reduce(f32[16]{0:T(128)S(1)} %get-tuple-element.30), channel_id=1, replica_groups=mesh['ta'=4,'gz'=8,'xy'=8] {'ta','gz','xy'}, use_global_device_ids=true, to_apply=%region_17.18 | all-reduce | flops 16 | bytes 128 | tf_op jit(solution)/shard_map/psum | solution.py:40
  494.1 2.4 collective-permute-start.12
  497.6 3.0 collective-permute-done.13
  500.6 2.1 collective-permute-start.14
  506.3 2.2 collective-permute-done.16
  508.5 2.7 collective-permute-done.17
  515.5 75.2 %all-reduce.4 = (f32[16]{0:T(128)S(1)}, f32[16]{0:T(128)S(1)}) all-reduce(f32[16]{0:T(128)S(1)} %get-tuple-element.102, f32[16]{0:T(128)S(1)} %multiply_reduce_fusion.8), channel_id=1, replica_groups=mesh['ta'=4,'gz'=8,'xy'=8] {'ta','gz','xy'}, use_global_device_ids=true, to_apply=%region_21.22 | all-reduce | flops 32 | bytes 256 | tf_op jit(solution)/shard_map/psum | solution.py:105
  590.9 74.6 %all-reduce.3 = (f32[16]{0:T(128)S(1)}, f32[16]{0:T(128)S(1)}) all-reduce(f32[16]{0:T(128)S(1)} %get-tuple-element.8, f32[16]{0:T(128)S(1)} %get-tuple-element.7), channel_id=1, replica_groups=mesh['ta'=4,'gz'=8,'xy'=8] {'ta','gz','xy'}, use_global_device_ids=true, to_apply=%region_25.26 | all-reduce | flops 32 | bytes 256 | tf_op jit(solution)/shard_map/psum | solution.py:105
  665.7 73.4 %all-reduce.2 = (f32[16]{0:T(128)S(1)}, f32[16]{0:T(128)S(1)}) all-reduce(f32[16]{0:T(128)S(1)} %get-tuple-element.6, f32[16]{0:T(128)S(1)} %get-tuple-element.5), channel_id=1, replica_groups=mesh['ta'=4,'gz'=8,'xy'=8] {'ta','gz','xy'}, use_global_device_ids=true, to_apply=%region_29.30 | all-reduce | flops 32 | bytes 256 | tf_op jit(solution)/shard_map/psum | solution.py:105
  739.4 74.2 %psum.127 = f32[16]{0:T(128)S(1)} all-reduce(f32[16]{0:T(128)S(1)} %multiply_reduce_fusion.3), channel_id=1, replica_groups=mesh['ta'=4,'gz'=8,'xy'=8] {'ta','gz','xy'}, use_global_device_ids=true, to_apply=%region_31.32 | all-reduce | flops 16 | bytes 128 | tf_op jit(solution)/shard_map/psum | solution.py:40
  814.5 8.8 %custom-call.9 = f32[16,6,6]{2,1,0:T(8,128)S(1)} custom-call(f32[16,6,6]{2,1,0:T(8,128)S(1)} %fusion.88), custom_call_target="Cholesky" | custom-call | tf_op jit(solution)/shard_map/jit(cholesky)/cholesky | solution.py:82
  823.6 7.6 custom-call.10
  (150 shorter events, 37.2 us)
Async XLA Ops:
  0.0 100.2 %copy-start = (bf16[2,2,2,2,9,64,128]{6,5,4,3,2,1,0:T(8,128)(2,1)S(1)}, bf16[2,2,2,2,9,64,128]{6,5,4,3,2,1,0:T(8,128)(2,1)}, u32[]{:S(2)}) copy-start(bf16[2,2,2,2,9,64,128]{6,5,4,3,2,1,0:T(8,128)(2,1)} %param.3) | copy-start | bytes 7077892
  83.5 2.8 collective-permute-start
  84.1 4.0 collective-permute-start.1
  88.1 5.2 collective-permute-start.2
  90.2 3.1 collective-permute-start.3
  93.3 3.9 collective-permute-start.4
  94.0 5.0 collective-permute-start.5
  100.2 1.2 copy-start.1
  250.9 3.4 collective-permute-start.6
  253.2 4.0 collective-permute-start.7
  257.2 3.7 collective-permute-start.8
  259.4 1.6 collective-permute-start.9
  261.0 3.9 collective-permute-start.10
  262.0 5.0 collective-permute-start.11
  494.1 3.4 collective-permute-start.12
  496.5 4.0 collective-permute-start.13
  500.6 3.7 collective-permute-start.14
  502.7 1.6 collective-permute-start.15
  504.3 4.2 collective-permute-start.16
  506.2 5.0 collective-permute-start.17
where the time goes:
time: 834 us; the launch traced here: 833 us
  blocking collectives  750 us (90%)
  waiting for transfers between devices  28.3 us (3%)
  other arithmetic  27.2 us (3%)
  starting transfers between devices  18.8 us (2%)
    psum x6, blocking collectives, on_device(): lax.psum(inner_pair(basis[earlier], residue), ('ta', 'gz', 'xy'))  447 us
    psum x4, blocking collectives, global_squares(): lax.psum(jnp.sum(field * field, axis=(0, 1, 2, 3, 5)), ('ta', 'gz', 'xy'))  303 us
  transfers between devices with their start and end apart: 18, of which 15 were waited for; matrix products, arithmetic and copies ran while one was open for 0% of the time, Pallas kernels for 0%

commit v1 on v0

--- a/solution.py
+++ b/solution.py
@@ -37,7 +37,12 @@
 
 
 def global_squares(field):
-    return lax.psum(jnp.sum(field * field, axis=(0, 1, 2, 3, 5)), ("ta", "gz", "xy"))
+
+    def solve_values(x_in, link_axis):
+        vec_out = jax.lax.all_gather(x_in, link_axis).sum(axis=0)
+        return vec_out
+
+    return solve_values(jnp.sum(field * field, axis=(0, 1, 2, 3, 5)), link_axis=("ta", "gz", "xy"))
 
 
 def hop_products(padded, blocks, half):

time: 834 us -> 836 us (level)
    unnamed x0 -> x4, blocking collectives: none -> 303 us
    psum x4 -> x0, blocking collectives: 303 us -> none  [global_squares(): lax.psum(jnp.sum(field * field, axis=(0, 1, 2, 3, 5)), ('ta', 'gz', 'xy'))]
where the time goes in v1:
time: 836 us; the launch traced here: 835 us
  blocking collectives  750 us (90%)
  waiting for transfers between devices  28.3 us (3%)
  other arithmetic  27.5 us (3%)
  starting transfers between devices  18.9 us (2%)
    psum x6, blocking collectives, on_device(): lax.psum(inner_pair(basis[earlier], residue), ('ta', 'gz', 'xy'))  447 us
    unnamed x4, blocking collectives  303 us
  transfers between devices with their start and end apart: 18, of which 15 were waited for; matrix products, arithmetic and copies ran while one was open for 0% of the time, Pallas kernels for 0%

profile of v1, /device:TPU:1, one launch (start us, length us, event | category | flops | bytes accessed | tf_op | source)
XLA Modules:
  0.0 834.6 jit_solution(9074701247139356117)
XLA Ops:
  1.4 81.4 %all-reduce.2 = f32[4096]{0:T(1024)S(1)} all-reduce(f32[4096]{0:T(1024)S(1)} %dynamic-update-slice.3), channel_id=2, replica_groups=mesh['ta'=4,'gz'=8,'xy'=8] {'ta','gz','xy'}, use_global_device_ids=true, to_apply=%add.2 | all-reduce | flops 4096 | bytes 32768
  88.5 2.1 collective-permute-start.2
  95.4 2.3 collective-permute-done.4
  102.6 74.0 %all-reduce.11 = (f32[16]{0:T(128)S(1)}, f32[16]{0:T(128)S(1)}) all-reduce(f32[16]{0:T(128)S(1)} %multiply_reduce_fusion.2, f32[16]{0:T(128)S(1)} %get-tuple-element.74), channel_id=1, replica_groups=mesh['ta'=4,'gz'=8,'xy'=8] {'ta','gz','xy'}, use_global_device_ids=true, to_apply=%region_5.6 | all-reduce | flops 32 | bytes 256 | tf_op jit(solution)/shard_map/psum | solution.py:110
  177.1 74.4 %all-reduce.3 = f32[4096]{0:T(1024)S(1)} all-reduce(f32[4096]{0:T(1024)S(1)} %dynamic-update-slice.4), channel_id=3, replica_groups=mesh['ta'=4,'gz'=8,'xy'=8] {'ta','gz','xy'}, use_global_device_ids=true, to_apply=%add.3 | all-reduce | flops 4096 | bytes 32768
  251.8 2.4 collective-permute-start.6
  255.2 3.0 collective-permute-done.7
  258.2 2.1 collective-permute-start.8
  263.5 2.3 collective-permute-done.10
  265.8 2.1 collective-permute-done.11
  270.6 75.2 %all-reduce.10 = (f32[16]{0:T(128)S(1)}, f32[16]{0:T(128)S(1)}) all-reduce(f32[16]{0:T(128)S(1)} %get-tuple-element.100, f32[16]{0:T(128)S(1)} %multiply_reduce_fusion.12), channel_id=1, replica_groups=mesh['ta'=4,'gz'=8,'xy'=8] {'ta','gz','xy'}, use_global_device_ids=true, to_apply=%region_11.12 | all-reduce | flops 32 | bytes 256 | tf_op jit(solution)/shard_map/psum | solution.py:110
  347.0 74.4 %all-reduce.9 = (f32[16]{0:T(128)S(1)}, f32[16]{0:T(128)S(1)}) all-reduce(f32[16]{0:T(128)S(1)} %get-tuple-element.10, f32[16]{0:T(128)S(1)} %get-tuple-element.9), channel_id=1, replica_groups=mesh['ta'=4,'gz'=8,'xy'=8] {'ta','gz','xy'}, use_global_device_ids=true, to_apply=%region_15.16 | all-reduce | flops 32 | bytes 256 | tf_op jit(solution)/shard_map/psum | solution.py:110
  421.8 73.4 %all-reduce.4 = f32[4096]{0:T(1024)S(1)} all-reduce(f32[4096]{0:T(1024)S(1)} %dynamic-update-slice.5), channel_id=4, replica_groups=mesh['ta'=4,'gz'=8,'xy'=8] {'ta','gz','xy'}, use_global_device_ids=true, to_apply=%add.4 | all-reduce | flops 4096 | bytes 32768
  495.5 2.4 collective-permute-start.12
  499.0 3.0 collective-permute-done.13
  502.0 2.1 collective-permute-start.14
  507.7 2.2 collective-permute-done.16
  510.0 2.7 collective-permute-done.17
  516.9 75.2 %all-reduce.8 = (f32[16]{0:T(128)S(1)}, f32[16]{0:T(128)S(1)}) all-reduce(f32[16]{0:T(128)S(1)} %get-tuple-element.102, f32[16]{0:T(128)S(1)} %multiply_reduce_fusion.8), channel_id=1, replica_groups=mesh['ta'=4,'gz'=8,'xy'=8] {'ta','gz','xy'}, use_global_device_ids=true, to_apply=%region_21.22 | all-reduce | flops 32 | bytes 256 | tf_op jit(solution)/shard_map/psum | solution.py:110
  592.4 74.6 %all-reduce.7 = (f32[16]{0:T(128)S(1)}, f32[16]{0:T(128)S(1)}) all-reduce(f32[16]{0:T(128)S(1)} %get-tuple-element.8, f32[16]{0:T(128)S(1)} %get-tuple-element.7), channel_id=1, replica_groups=mesh['ta'=4,'gz'=8,'xy'=8] {'ta','gz','xy'}, use_global_device_ids=true, to_apply=%region_25.26 | all-reduce | flops 32 | bytes 256 | tf_op jit(solution)/shard_map/psum | solution.py:110
  667.2 73.4 %all-reduce.6 = (f32[16]{0:T(128)S(1)}, f32[16]{0:T(128)S(1)}) all-reduce(f32[16]{0:T(128)S(1)} %get-tuple-element.6, f32[16]{0:T(128)S(1)} %get-tuple-element.5), channel_id=1, replica_groups=mesh['ta'=4,'gz'=8,'xy'=8] {'ta','gz','xy'}, use_global_device_ids=true, to_apply=%region_29.30 | all-reduce | flops 32 | bytes 256 | tf_op jit(solution)/shard_map/psum | solution.py:110
  741.1 74.3 %all-reduce.5 = f32[4096]{0:T(1024)S(1)} all-reduce(f32[4096]{0:T(1024)S(1)} %dynamic-update-slice.6), channel_id=5, replica_groups=mesh['ta'=4,'gz'=8,'xy'=8] {'ta','gz','xy'}, use_global_device_ids=true, to_apply=%add.5 | all-reduce | flops 4096 | bytes 32768
  816.4 8.8 %custom-call.9 = f32[16,6,6]{2,1,0:T(8,128)S(1)} custom-call(f32[16,6,6]{2,1,0:T(8,128)S(1)} %fusion.88), custom_call_target="Cholesky" | custom-call | tf_op jit(solution)/shard_map/jit(cholesky)/cholesky | solution.py:87
  825.5 7.6 custom-call.10
  (166 shorter events, 38.9 us)
Async XLA Ops:
  0.0 100.6 %copy-start = (bf16[2,2,2,2,9,64,128]{6,5,4,3,2,1,0:T(8,128)(2,1)S(1)}, bf16[2,2,2,2,9,64,128]{6,5,4,3,2,1,0:T(8,128)(2,1)}, u32[]{:S(2)}) copy-start(bf16[2,2,2,2,9,64,128]{6,5,4,3,2,1,0:T(8,128)(2,1)} %param.3) | copy-start | bytes 7077892
  83.9 2.8 collective-permute-start
  84.5 4.0 collective-permute-start.1
  88.5 5.2 collective-permute-start.2
  90.7 3.0 collective-permute-start.3
  93.8 3.9 collective-permute-start.4
  94.4 5.0 collective-permute-start.5
  100.6 1.2 copy-start.1
  251.8 3.4 collective-permute-start.6
  254.1 4.0 collective-permute-start.7
  258.2 3.7 collective-permute-start.8
  260.3 1.6 collective-permute-start.9
  261.9 3.9 collective-permute-start.10
  262.9 5.0 collective-permute-start.11
  495.5 3.5 collective-permute-start.12
  498.0 4.0 collective-permute-start.13
  502.0 3.7 collective-permute-start.14
  504.1 1.6 collective-permute-start.15
  505.8 4.2 collective-permute-start.16
  507.6 5.0 collective-permute-start.17
